TPU v7x, 256 devices: a whole 4x4x8 slice. The times are simulated.
256 devices in a mesh: win: 4 (over z_lo), rcv: 64 (over x, z_hi, y, core).
Axes of the slice: x: 4, y: 4, z: 8 (z_hi: 2, z_lo: 4; z = z_hi * 4 + z_lo), core: 2. Of those that a mesh axis runs over, the one named last changes fastest.
Arguments:
- spectra: bfloat16 [4096, 16, 2, 1024], P('rcv', 'win'), may hold values from -6 to 6
- source_block: int32 [1], replicated, may hold values from 0 to 63
Outputs:
- correlations: bfloat16 [4096, 64, 2048], P('rcv', None, 'win')
All inputs are finite; a program needn't handle non-finite values.
Results may differ from a plain program's by a relative error of at most 0.015.
Values may be sent and summed in bfloat16 or wider, within the bound.
No kernel may reach another device: no remote copies, remote signals or barrier semaphores. Data moves between devices by JAX's collectives and lax.ppermute only.
A program may use at most 256 MiB of HBM per device.

v0:
```python
import math

import jax
import jax.numpy as jnp
from jax import lax
from jax.sharding import PartitionSpec as P


def broadcast(shard, axis, root):
    mine = lax.axis_index(axis) == root
    return lax.psum(jnp.where(mine, shard, jnp.zeros_like(shard)), axis)


def cross_terms(receivers, source):
    flipped = jnp.stack([-receivers[:, :, 1], receivers[:, :, 0]], axis=2)
    real_part = jnp.einsum("rwcf,swcf->rsf", receivers, source, preferred_element_type=jnp.float32)
    imag_part = jnp.einsum("rwcf,swcf->rsf", flipped, source, preferred_element_type=jnp.float32)
    return jnp.stack([real_part, imag_part], axis=2)


def lag_table(n_freqs):
    n_lags = 2 * n_freqs
    freq_index = jnp.arange(n_freqs, dtype=jnp.int32)
    lag_index = jnp.arange(n_lags, dtype=jnp.int32) - n_freqs
    phase_index = freq_index[:, None] * lag_index[None, :] % n_lags
    angle = 2.0 * math.pi / n_lags * phase_index.astype(jnp.float32)
    return jnp.concatenate([jnp.cos(angle), -jnp.sin(angle)], axis=0).astype(jnp.bfloat16)


def to_lags(cross_spec, lag_scale, table):
    row_count, source_count, two_parts, n_freqs = cross_spec.shape
    flat_spec = cross_spec.astype(jnp.bfloat16).reshape(
        row_count * source_count, two_parts * n_freqs
    )
    lagged = jnp.dot(flat_spec, table, preferred_element_type=jnp.float32) * lag_scale
    return lagged.astype(jnp.bfloat16).reshape(row_count, source_count, table.shape[1])


def body(spectra, source_block):
    root_index = source_block[0]
    win_count = lax.axis_size("win")
    n_freqs = spectra.shape[3]
    lag_scale = 1.0 / math.sqrt(2 * n_freqs * spectra.shape[1] * win_count)
    table = lag_table(n_freqs)
    receivers = lax.all_to_all(spectra, "win", split_axis=0, concat_axis=1, tiled=True)
    whole_block = lax.all_gather(spectra, "win", axis=1, tiled=True)
    source = broadcast(whole_block, "rcv", root_index)
    cross_spec = cross_terms(receivers, source)
    lagged = to_lags(cross_spec, lag_scale, table)
    return lax.all_to_all(lagged, "win", split_axis=2, concat_axis=0, tiled=True)


def solution(mesh):
    in_specs = (P("rcv", "win", None, None), P())
    out_specs = P("rcv", None, "win")
    return jax.shard_map(body, mesh=mesh, in_specs=in_specs, out_specs=out_specs, check_vma=False)
```

profile of v0, /device:TPU:1, one launch (start us, length us, event | category | flops | bytes accessed | tf_op | source)
XLA Modules:
  0.0 1127.5 jit_solution(3235380185122393054)
XLA Ops:
  6.5 0.0 all-gather.2.cloned.1.call-start
  6.5 2.8 copy.31
  9.3 0.0 all-gather.2.cloned.1.call-update
  9.3 0.0 all-reduce.2.cloned.1.call-start
  10.0 87.2 %all-gather.2.cloned.1.call-done = bf16[64,16,2,1024]{3,0,2,1:T(8,128)(2,1)} async-done(((bf16[64,4,2,1024]{3,0,2,1:T(8,128)(2,1)}), bf16[64,16,2,1024]{3,0,2,1:T(8,128)(2,1)}) %all-gather.2.cloned.1.call-update) | async-done | bytes 4194320 | tf_op jit(solution)/shard_map/all_gather | solution.py:46
  97.2 12.9 %copy.32 = bf16[64,16,2,1024]{0,1,2,3:T(8,128)(2,1)} copy(bf16[64,16,2,1024]{3,0,2,1:T(8,128)(2,1)} %all-gather.2.cloned.1.call-done) | data formatting | bytes 8388608 | tf_op jit(solution)/shard_map/all_gather | solution.py:46
  110.1 3.8 broadcast_select_fusion
  113.9 0.0 all-reduce.2.cloned.1.call-update
  114.0 3.7 all-to-all-start
  117.7 35.0 %cosine_convert_fusion = (bf16[1024,2048]{1,0:T(8,128)(2,1)}, bf16[1024,2048]{1,0:T(8,128)(2,1)}) fusion(s32[2048]{0:T(1024)S(1)} %iota_add_fusion), kind=kLoop, calls=%fused_computation.19 | loop fusion | flops 35651584 | bytes 8396800 | tf_op jit(solution)/shard_map/convert
  152.7 0.0 all-to-all-done
  152.7 0.6 copy.33
  153.3 0.1 copy.34
  153.4 12.2 %copy.35 = bf16[16,16,2,1024]{1,0,2,3:T(8,128)(2,1)} copy(bf16[16,16,2,1024]{3,0,2,1:T(8,128)(2,1)S(1)} %bitcast.42) | data formatting | bytes 2097152 | tf_op jit(solution)/shard_map/all_to_all | solution.py:45
  165.6 6.0 slice_negate_fusion
  171.6 760.1 %all-reduce.2.cloned.1.call-done = bf16[64,16,2,1024]{0,1,2,3:T(8,128)(2,1)} async-done(((bf16[64,16,2,1024]{0,1,2,3:T(8,128)(2,1)}), bf16[64,16,2,1024]{0,1,2,3:T(8,128)(2,1)}) %all-reduce.2.cloned.1.call-update) | async-done | bytes 4194320 | tf_op jit(solution)/shard_map/psum | solution.py:11
  931.7 8.2 fusion.16
  939.9 10.2 fusion.17
  950.1 7.3 pad_maximum_fusion
  957.4 11.9 %reshape.13 = bf16[1024,2048]{0,1:T(8,128)(2,1)} reshape(bf16[16,64,2,1024]{1,0,3,2:T(8,128)(2,1)} %pad_maximum_fusion) | data formatting | bytes 8388608 | tf_op jit(solution)/shard_map/convert_element_type | solution.py:32
  969.3 14.0 %multiply_convert_fusion = bf16[1024,2048]{1,0:T(8,128)(2,1)} fusion(bf16[1024,2048]{0,1:T(8,128)(2,1)} %reshape.13, bf16[1024,2048]{1,0:T(8,128)(2,1)} %get-tuple-element.8, bf16[1024,2048]{1,0:T(8,128)(2,1)} %get-tuple-element.7), kind=kOutput, calls=%fused_computation.17 | convolution fusion | flops 8610906112 | bytes 16777216 | tf_op jit(solution)/shard_map/dot_general | solution.py:35
  983.3 10.9 copy.39
  994.2 9.5 reshape.14
  1003.7 97.9 %all_to_all.36 = bf16[4,2,262144]{2,1,0:T(2,128)(2,1)} all-to-all(bf16[4,2,262144]{2,1,0:T(2,128)(2,1)} %reshape.14), channel_id=1, replica_groups=mesh['win'=4,'rcv'=64] {'win'}, dimensions={0} | all-to-all | bytes 8388608 | tf_op jit(solution)/shard_map/all_to_all | solution.py:50
  1101.6 9.3 reshape.15
  1110.9 9.7 copy.40
  (1 shorter events, 0.0 us)
Async XLA Ops:
  6.5 90.7 %all-gather.2.cloned.1.call-start = ((), (), s32[]{:S(2)}) async-start(), calls=%async_computation.2 | async-start | bytes 5242880 | tf_op jit(solution)/shard_map/all_gather | solution.py:46
  9.3 922.3 %all-reduce.2.cloned.1.call-start = ((), (), s32[]{:S(2)}) async-start(), calls=%async_computation.3 | async-start | bytes 16777216 | tf_op jit(solution)/shard_map/psum | solution.py:11
  114.0 38.8 %all-to-all-start = ((bf16[64,4,2,1024]{3,2,1,0:T(2,128)(2,1)}), bf16[64,4,2,1024]{3,2,1,0:T(2,128)(2,1)S(1)}, u32[]{:S(2)}, u32[]{:S(2)}) async-start(bf16[64,4,2,1024]{3,2,1,0:T(2,128)(2,1)} %param.2), calls=%async_computation | async-start | bytes 2097152 | tf_op jit(solution)/shard_map/all_to_all | solution.py:45
Sparse Core Ops, SparseCore 0:
  9.5 87.7 all-gather.1
  114.1 817.5 all-reduce.1
where the time goes:
time: 1130 us
  waiting for transfers between devices  847 us (75%)
  blocking collectives  97.9 us (9%)
  local copies, waits for them, and re-layouts  79.9 us (7%)
  other arithmetic  52.1 us (5%)
  matrix products  32.4 us (3%)
  between operations  14.1 us (1%)
    psum x1, waiting for transfers between devices, broadcast(): return lax.psum(jnp.where(mine, shard, jnp.zeros_like(shard)), axis)  760 us
    all_to_all x1, blocking collectives, body(): lax.all_to_all(lagged, 'win', split_axis=2, concat_axis=0, tiled=True)  97.9 us
    all_gather x1, waiting for transfers between devices, body(): whole_block = lax.all_gather(spectra, 'win', axis=1, tiled=True)  87.2 us
    another operation x1, other arithmetic  35 us
  transfers between devices with their start and end apart: 3, of which 2 were waited for; matrix products, arithmetic and copies ran while one was open for 5% of the time, Pallas kernels for 0%

commit v1 on v0

v1 whole, which is shorter than its diff:
```python
import math

import jax
import jax.numpy as jnp
from jax import lax
from jax.sharding import PartitionSpec as P

RCV_DIMS = (("x", 16, 4), ("z_hi", 8, 2), ("y", 2, 4), ("core", 1, 2))


def coord(index, stride, size):
    return (index // stride) % size


def shifted(stride, size, step, n):
    pairs = []
    for i in range(n):
        c = (i // stride) % size
        pairs.append((i, i + (((c + step) % size) - c) * stride))
    return pairs


def ring_broadcast(held, me, root, stride, size, n):
    dist = (coord(me, stride, size) - coord(root, stride, size)) % size
    if size == 2:
        got = lax.ppermute(held, "rcv", shifted(stride, size, 1, n))
        return jnp.where(dist == 1, got, held)
    from_below = lax.ppermute(held, "rcv", shifted(stride, size, 1, n))
    from_above = lax.ppermute(held, "rcv", shifted(stride, size, -1, n))
    held = jnp.where(dist == 1, from_below, jnp.where(dist == size - 1, from_above, held))
    for d in range(2, size // 2 + 1):
        got = lax.ppermute(held, "rcv", shifted(stride, size, 1, n))
        held = jnp.where(dist == d, got, held)
    return held


def source_half(spectra, root):
    n = lax.axis_size("rcv")
    me = lax.axis_index("rcv")
    core = me % 2
    partner = lax.ppermute(spectra, "rcv", shifted(1, 2, 1, n))
    held = jnp.where(core == root % 2, spectra, partner)
    halves = held.reshape((2, held.shape[0] // 2) + held.shape[1:])
    half = lax.dynamic_index_in_dim(halves, core, 0, keepdims=False)
    for name, stride, size in RCV_DIMS[:-1]:
        half = ring_broadcast(half, me, root, stride, size, n)
    return half


def cross_terms(receivers, source):
    flipped = jnp.stack([-receivers[:, :, 1], receivers[:, :, 0]], axis=2)
    real_part = jnp.einsum("rwcf,swcf->rsf", receivers, source, preferred_element_type=jnp.float32)
    imag_part = jnp.einsum("rwcf,swcf->rsf", flipped, source, preferred_element_type=jnp.float32)
    return jnp.stack([real_part, imag_part], axis=2)


def lag_table(n_freqs, lag_start, n_lags):
    freq_index = jnp.arange(n_freqs, dtype=jnp.int32)
    lag_index = jnp.arange(n_lags, dtype=jnp.int32) + lag_start
    phase_index = freq_index[:, None] * lag_index[None, :] % (2 * n_freqs)
    angle = math.pi / n_freqs * phase_index.astype(jnp.float32)
    return jnp.concatenate([jnp.cos(angle), -jnp.sin(angle)], axis=0).astype(jnp.bfloat16)


def body(spectra, source_block):
    root = source_block[0]
    win_count = lax.axis_size("win")
    n_freqs = spectra.shape[3]
    all_lags = 2 * n_freqs
    my_lags = all_lags // win_count
    lag_scale = 1.0 / math.sqrt(all_lags * spectra.shape[1] * win_count)
    lag_start = lax.axis_index("win") * my_lags - n_freqs
    table = lag_table(n_freqs, lag_start, my_lags)

    receivers = lax.all_gather(spectra, "win", axis=1, tiled=True)
    half = source_half(spectra, root)
    half = lax.all_gather(half, "win", axis=1, tiled=True)
    other = lax.ppermute(half, "rcv", shifted(1, 2, 1, lax.axis_size("rcv")))
    first = lax.axis_index("rcv") % 2 == 0
    source = jnp.concatenate(
        [jnp.where(first, half, other), jnp.where(first, other, half)], axis=0
    )

    cross_spec = cross_terms(receivers, source).astype(jnp.bfloat16)
    rows, sources = cross_spec.shape[:2]
    flat_spec = cross_spec.reshape(rows * sources, 2 * n_freqs)
    lagged = jnp.dot(flat_spec, table, preferred_element_type=jnp.float32) * lag_scale
    return lagged.astype(jnp.bfloat16).reshape(rows, sources, my_lags)


def solution(mesh):
    in_specs = (P("rcv", "win", None, None), P())
    out_specs = P("rcv", None, "win")
    return jax.shard_map(body, mesh=mesh, in_specs=in_specs, out_specs=out_specs, check_vma=False)
```

time: 1130 us -> 437 us (0.39)
  waiting for transfers between devices: 847 us -> 194 us
  blocking collectives: 97.9 us -> 0 us
  local copies, waits for them, and re-layouts: 79.9 us -> 113 us
  matrix products: 32.4 us -> 51.7 us
    psum x1 -> x0, waiting for transfers between devices: 760 us -> none  [broadcast(): return lax.psum(jnp.where(mine, shard, jnp.zeros_like(shard)), axis)]
    all_to_all x1 -> x0, blocking collectives: 97.9 us -> none  [body(): lax.all_to_all(lagged, 'win', split_axis=2, concat_axis=0, tiled=True)]
    ppermute x0 -> x9, waiting for transfers between devices: none -> 64.9 us  [the longest x3 41.2 us: ring_broadcast(): got = lax.ppermute(held, 'rcv', shifted(stride, size, 1, n))]
    another operation x0 -> x1, local copies, waits for them, and re-layouts: none -> 54.5 us  [cross_terms(): return jnp.stack([real_part, imag_part], axis=2)]
    all_gather x1 -> x2, waiting for transfers between devices: 87.2 us -> 129 us  [the longest x1 71.2 us: body(): receivers = lax.all_gather(spectra, 'win', axis=1, tiled=True)]
    another operation x1, other arithmetic: 35 us -> 9.29 us
    all_to_all x4 -> x0, local copies, waits for them, and re-layouts: 22.6 us -> none  [the longest x3 12.9 us: body(): lax.all_to_all(spectra, 'win', split_axis=0, concat_axis=1, tiled=True)]
    all_gather x1 -> x3, local copies, waits for them, and re-layouts: 12.9 us -> 29.2 us  [the longest x2 16.2 us: body(): half = lax.all_gather(half, 'win', axis=1, tiled=True)]
  transfers between devices with their start and end apart: 3 -> 11, of which waited for: 2 -> 8; matrix products, arithmetic and copies ran while one was open for 5% -> 11% of each run, Pallas kernels for 0% -> 0%
where the time goes in v1:
time: 437 us; the launch traced here: 438 us
  waiting for transfers between devices  194 us (44%)
  local copies, waits for them, and re-layouts  113 us (26%)
  matrix products  51.7 us (12%)
  other arithmetic  50.2 us (11%)
  starting transfers between devices  14.9 us (3%)
  between operations  14.2 us (3%)
    all_gather x1, waiting for transfers between devices, body(): receivers = lax.all_gather(spectra, 'win', axis=1, tiled=True)  71.2 us
    all_gather x1, waiting for transfers between devices, body(): half = lax.all_gather(half, 'win', axis=1, tiled=True)  57.9 us
    another operation x1, local copies, waits for them, and re-layouts, cross_terms(): return jnp.stack([real_part, imag_part], axis=2)  54.5 us
    ppermute x3, waiting for transfers between devices, ring_broadcast(): got = lax.ppermute(held, 'rcv', shifted(stride, size, 1, n))  41.2 us
    another operation x1, other arithmetic, cross_terms(): return jnp.stack([real_part, imag_part], axis=2)  22.7 us
    ppermute x2, waiting for transfers between devices, ring_broadcast(): from_below = lax.ppermute(held, 'rcv', shifted(stride, size, 1, n))  21.8 us
    dot_general x1, matrix products, cross_terms(): jnp.einsum('rwcf,swcf->rsf', flipped, source, preferred_element_type=jnp....  20.5 us
    dot_general x1, matrix products, cross_terms(): jnp.einsum('rwcf,swcf->rsf', receivers, source, preferred_element_type=jn...  20.5 us
  transfers between devices with their start and end apart: 11, of which 8 were waited for; matrix products, arithmetic and copies ran while one was open for 11% of the time, Pallas kernels for 0%

profile of v1, /device:TPU:1, one launch (start us, length us, event | category | flops | bytes accessed | tf_op | source)
XLA Modules:
  0.0 437.9 jit_solution(5012104868404308723)
XLA Ops:
  6.5 0.0 copy-start.2
  6.5 0.0 all-gather.3.cloned.1.call-start
  6.5 3.2 collective-permute-start
  10.5 1.8 collective-permute-done
  12.3 1.3 broadcast_select_fusion.2
  13.6 0.4 constant_dynamic-slice_fusion
  14.1 0.3 copy.26
  14.4 0.1 collective-permute-start.1
  14.5 2.7 collective-permute-start.2
  17.1 11.8 %collective-permute-done.1 = bf16[32,4,2,1024]{3,0,2,1:T(8,128)(2,1)S(1)} collective-permute-done((bf16[32,4,2,1024]{3,0,2,1:T(8,128)(2,1)S(1)}, bf16[32,4,2,1024]{3,0,2,1:T(8,128)(2,1)S(1)}, u32[]{:S(2)}, u32[]{:S(2)}) %collective-permute-start.1) | collective-permute-done | bytes 524320 | tf_op jit(solution)/shard_map/ppermute | solution.py:28
  28.9 0.0 collective-permute-done.2
  28.9 0.6 select_select_fusion.1
  29.5 0.1 collective-permute-start.3
  29.6 15.1 %collective-permute-done.3 = bf16[32,4,2,1024]{3,0,2,1:T(8,128)(2,1)S(1)} collective-permute-done((bf16[32,4,2,1024]{3,0,2,1:T(8,128)(2,1)S(1)}, bf16[32,4,2,1024]{3,0,2,1:T(8,128)(2,1)S(1)}, u32[]{:S(2)}, u32[]{:S(2)}) %collective-permute-start.3) | collective-permute-done | bytes 524320 | tf_op jit(solution)/shard_map/ppermute | solution.py:32
  44.7 0.1 broadcast_select_fusion.3
  44.8 4.9 %collective-permute-start.4 = (bf16[32,4,2,1024]{3,0,2,1:T(8,128)(2,1)S(1)}, bf16[32,4,2,1024]{3,0,2,1:T(8,128)(2,1)S(1)}, u32[]{:S(2)}, u32[]{:S(2)}) collective-permute-start(bf16[32,4,2,1024]{3,0,2,1:T(8,128)(2,1)S(1)} %broadcast_select_fusion.3), channel_id=1, source_target_pairs={{0,8},{1,9},{2,10},{3,11},{4,12},{5,13},{6,14},{7,15},{8,0},{9,1},... | collective-permute-start | bytes 1572872 | tf_op jit(solution)/shard_map/ppermute | solution.py:26
  49.7 14.4 %collective-permute-done.4 = bf16[32,4,2,1024]{3,0,2,1:T(8,128)(2,1)S(1)} collective-permute-done((bf16[32,4,2,1024]{3,0,2,1:T(8,128)(2,1)S(1)}, bf16[32,4,2,1024]{3,0,2,1:T(8,128)(2,1)S(1)}, u32[]{:S(2)}, u32[]{:S(2)}) %collective-permute-start.4) | collective-permute-done | bytes 524320 | tf_op jit(solution)/shard_map/ppermute | solution.py:26
  64.1 0.1 broadcast_select_fusion.4
  64.2 0.1 collective-permute-start.5
  64.3 2.6 collective-permute-start.6
  66.9 10.0 %collective-permute-done.5 = bf16[32,4,2,1024]{3,0,2,1:T(8,128)(2,1)S(1)} collective-permute-done((bf16[32,4,2,1024]{3,0,2,1:T(8,128)(2,1)S(1)}, bf16[32,4,2,1024]{3,0,2,1:T(8,128)(2,1)S(1)}, u32[]{:S(2)}, u32[]{:S(2)}) %collective-permute-start.5) | collective-permute-done | bytes 524320 | tf_op jit(solution)/shard_map/ppermute | solution.py:28
  76.9 0.0 collective-permute-done.6
  76.9 0.1 select_select_fusion
  77.0 0.1 collective-permute-start.7
  77.1 11.8 %collective-permute-done.7 = bf16[32,4,2,1024]{3,0,2,1:T(8,128)(2,1)S(1)} collective-permute-done((bf16[32,4,2,1024]{3,0,2,1:T(8,128)(2,1)S(1)}, bf16[32,4,2,1024]{3,0,2,1:T(8,128)(2,1)S(1)}, u32[]{:S(2)}, u32[]{:S(2)}) %collective-permute-start.7) | collective-permute-done | bytes 524320 | tf_op jit(solution)/shard_map/ppermute | solution.py:32
  88.9 0.9 broadcast_select_fusion.5
  89.7 0.0 all-gather.3.cloned.1.call-update
  89.8 0.0 all-gather.5.cloned.1.call-start
  89.8 0.0 copy-done.2
  89.8 1.5 copy.14
  91.4 0.0 all-gather.5.cloned.1.call-update
  91.4 57.9 %all-gather.3.cloned.1.call-done = bf16[32,16,2,1024]{3,0,2,1:T(8,128)(2,1)} async-done(((bf16[32,4,2,1024]{3,0,2,1:T(8,128)(2,1)}), bf16[32,16,2,1024]{3,0,2,1:T(8,128)(2,1)}) %all-gather.3.cloned.1.call-update) | async-done | bytes 2097168 | tf_op jit(solution)/shard_map/all_gather | solution.py:77
  149.3 4.1 copy.9
  153.4 1.0 collective-permute-start.8
  154.4 9.3 %cosine_convert_fusion = (bf16[1024,512]{1,0:T(8,128)(2,1)S(1)}, bf16[1024,512]{1,0:T(8,128)(2,1)}) fusion(s32[512]{0:T(512)S(1)} %iota_add_fusion), kind=kLoop, calls=%fused_computation.23 | loop fusion | flops 8912896 | bytes 2099200 | tf_op jit(solution)/shard_map/convert
  163.6 71.2 %all-gather.5.cloned.1.call-done = bf16[64,16,2,1024]{3,0,2,1:T(8,128)(2,1)} async-done(((bf16[64,4,2,1024]{3,0,2,1:T(8,128)(2,1)}), bf16[64,16,2,1024]{3,0,2,1:T(8,128)(2,1)}) %all-gather.5.cloned.1.call-update) | async-done | bytes 4194320 | tf_op jit(solution)/shard_map/all_gather | solution.py:75
  234.8 13.0 %copy.15 = bf16[64,16,2,1024]{0,1,2,3:T(8,128)(2,1)} copy(bf16[64,16,2,1024]{3,0,2,1:T(8,128)(2,1)} %all-gather.5.cloned.1.call-done) | data formatting | bytes 8388608 | tf_op jit(solution)/shard_map/all_gather | solution.py:75
  247.8 0.0 copy-start.1
  247.8 6.1 %slice_negate_fusion = (bf16[64,16,1,1024]{0,1,2,3:T(8,128)(2,1)}, bf16[64,16,1,1024]{0,1,2,3:T(8,128)(2,1)}) fusion(bf16[64,16,2,1024]{0,1,2,3:T(8,128)(2,1)} %copy.15), kind=kLoop, calls=%fused_computation.12 | loop fusion | flops 1048576 | bytes 8388608 | tf_op jit(solution)/shard_map/neg | solution.py:51
  253.9 0.0 copy-done.1
  253.9 12.2 %copy.10 = bf16[32,16,2,1024]{0,1,2,3:T(8,128)(2,1)} copy(bf16[32,16,2,1024]{3,0,2,1:T(8,128)(2,1)S(1)} %copy-done.1) | data formatting | bytes 4194304 | tf_op jit(solution)/shard_map/all_gather | solution.py:77
  266.1 0.0 collective-permute-done.8
  266.1 15.1 %copy.11 = bf16[32,16,2,1024]{0,1,2,3:T(8,128)(2,1)} copy(bf16[32,16,2,1024]{3,1,2,0:T(8,128)(2,1)} %collective-permute-done.8) | data formatting | bytes 4194304 | tf_op jit(solution)/shard_map/ppermute | solution.py:78
  281.2 9.1 %broadcast_select_fusion.1 = (bf16[32,16,2,1024]{0,1,2,3:T(8,128)(2,1)S(1)}, bf16[32,16,2,1024]{0,1,2,3:T(8,128)(2,1)}) fusion(bf16[32,16,2,1024]{0,1,2,3:T(8,128)(2,1)} %copy.10, bf16[32,16,2,1024]{0,1,2,3:T(8,128)(2,1)} %copy.11, pred[]{:T(512)S(6)} %eq.42), kind=kLoop, calls=%fused_computation.11 | loop fusion | flops 2097152 | bytes 8388609 | tf_op jit(solution)/shard_map/jit(_where)/select_n | solution.py:81
  290.3 0.0 copy-start
  290.3 20.5 %fusion = bf16[64,64,1,1024]{0,1,3,2:T(8,128)(2,1)} fusion(bf16[64,16,2,1024]{0,1,2,3:T(8,128)(2,1)} %copy.15, bf16[32,16,2,1024]{0,1,2,3:T(8,128)(2,1)} %get-tuple-element.6, bf16[32,16,2,1024]{0,1,2,3:T(8,128)(2,1)S(1)} %get-tuple-element.5), kind=kOutput, calls=%fused_computation.3 | convolution fusion | flops 281018368 | bytes 16777216 | tf_op jit(solution)/shard_map/rwcf,swcf->rsf/dot_general | solution.py:52
  310.8 0.0 copy-done
  310.8 20.5 %fusion.1 = bf16[64,64,1,1024]{0,1,3,2:T(8,128)(2,1)} fusion(bf16[64,16,1,1024]{0,1,2,3:T(8,128)(2,1)} %get-tuple-element.8, bf16[64,16,1,1024]{0,1,2,3:T(8,128)(2,1)} %get-tuple-element.7, bf16[32,16,2,1024]{0,1,2,3:T(8,128)(2,1)} %get-tuple-element.6, bf16[32,16,2,1024]{0,1,2,3:T(8,128)(2,1)} %copy-done), kind=kOutput, calls=%fused_computation.4 | convolution fusion | flops 283115520 | bytes 16777216 | tf_op jit(solution)/shard_map/rwcf,swcf->rsf/dot_general | solution.py:53
  331.4 22.7 %pad_maximum_fusion = bf16[64,64,2,1024]{0,1,3,2:T(8,128)(2,1)} fusion(bf16[64,64,1,1024]{0,1,3,2:T(8,128)(2,1)} %fusion.1, bf16[64,64,1,1024]{0,1,3,2:T(8,128)(2,1)} %fusion), kind=kLoop, calls=%fused_computation | loop fusion | flops 8388608 | bytes 33554432 | tf_op jit(solution)/shard_map/stack | solution.py:54
  354.1 54.5 %copy.18 = bf16[64,64,2,1024]{3,2,1,0:T(2,128)(2,1)} copy(bf16[64,64,2,1024]{0,1,3,2:T(8,128)(2,1)} %pad_maximum_fusion) | data formatting | bytes 33554432 | tf_op jit(solution)/shard_map/stack | solution.py:54
  408.6 0.0 copy-start.3
  408.6 11.8 %copy.22 = bf16[512,8,2,1024]{3,1,2,0:T(8,128)(2,1)S(1)} copy(bf16[512,8,2,1024]{3,2,1,0:T(2,128)(2,1)} %bitcast.38) | data formatting | bytes 33554432
  420.4 0.0 copy-done.3
  420.4 10.6 %multiply_convert_fusion = bf16[4096,512]{1,0:T(8,128)(2,1)} fusion(bf16[4096,2048]{1,0:T(8,128)(2,1)S(1)} %bitcast.39, bf16[1024,512]{1,0:T(8,128)(2,1)S(1)} %copy-done.3, bf16[1024,512]{1,0:T(8,128)(2,1)S(1)} %get-tuple-element.9), kind=kOutput, calls=%fused_computation.9 | convolution fusion | flops 8598323200 | bytes 23068672 | tf_op jit(solution)/shard_map/dot_general | solution.py:87
  (1 shorter events, 0.0 us)
Async XLA Ops:
  6.5 83.3 %copy-start.2 = (bf16[64,4,2,1024]{3,2,1,0:T(2,128)(2,1)S(1)}, bf16[64,4,2,1024]{3,2,1,0:T(2,128)(2,1)}, u32[]{:S(2)}) copy-start(bf16[64,4,2,1024]{3,2,1,0:T(2,128)(2,1)} %param.2) | copy-start | bytes 3145732
  6.5 142.8 %all-gather.3.cloned.1.call-start = ((), (), s32[]{:S(2)}) async-start(), calls=%async_computation | async-start | bytes 2621440 | tf_op jit(solution)/shard_map/all_gather | solution.py:77
  6.5 5.7 %collective-permute-start = (bf16[64,4,2,1024]{3,2,1,0:T(2,128)(2,1)}, bf16[64,4,2,1024]{3,2,1,0:T(2,128)(2,1)S(1)}, u32[]{:S(2)}, u32[]{:S(2)}) collective-permute-start(bf16[64,4,2,1024]{3,2,1,0:T(2,128)(2,1)} %param.2), channel_id=1, source_target_pairs={{0,1},{1,0},{2,3},{3,2},{4,5},{5,4},{6,7},{7,6},{8,9},{9,8},{10,11... | collective-permute-start | bytes 3145736 | tf_op jit(solution)/shard_map/ppermute | solution.py:41
  14.4 14.5 %collective-permute-start.1 = (bf16[32,4,2,1024]{3,0,2,1:T(8,128)(2,1)S(1)}, bf16[32,4,2,1024]{3,0,2,1:T(8,128)(2,1)S(1)}, u32[]{:S(2)}, u32[]{:S(2)}) collective-permute-start(bf16[32,4,2,1024]{3,0,2,1:T(8,128)(2,1)S(1)} %bitcast.43), channel_id=1, source_target_pairs={{0,16},{1,17},{2,18},{3,19},{4,20},{5,21},{6,22},{7,23},{8,24},{9,... | collective-permute-start | bytes 1572872 | tf_op jit(solution)/shard_map/ppermute | solution.py:28
  14.5 14.5 %collective-permute-start.2 = (bf16[32,4,2,1024]{3,0,2,1:T(8,128)(2,1)S(1)}, bf16[32,4,2,1024]{3,0,2,1:T(8,128)(2,1)S(1)}, u32[]{:S(2)}, u32[]{:S(2)}) collective-permute-start(bf16[32,4,2,1024]{3,0,2,1:T(8,128)(2,1)S(1)} %bitcast.44), channel_id=1, source_target_pairs={{0,48},{1,49},{2,50},{3,51},{4,52},{5,53},{6,54},{7,55},{8,56},{9,... | collective-permute-start | bytes 1572872 | tf_op jit(solution)/shard_map/ppermute | solution.py:29
  29.5 15.2 %collective-permute-start.3 = (bf16[32,4,2,1024]{3,0,2,1:T(8,128)(2,1)S(1)}, bf16[32,4,2,1024]{3,0,2,1:T(8,128)(2,1)S(1)}, u32[]{:S(2)}, u32[]{:S(2)}) collective-permute-start(bf16[32,4,2,1024]{3,0,2,1:T(8,128)(2,1)S(1)} %select_select_fusion.1), channel_id=1, source_target_pairs={{0,16},{1,17},{2,18},{3,19},{4,20},{5,21},{6,22},{7,23},{8,24},{9,... | collective-permute-start | bytes 1572872 | tf_op jit(solution)/shard_map/ppermute | solution.py:32
  44.8 19.3 %collective-permute-start.4 = (bf16[32,4,2,1024]{3,0,2,1:T(8,128)(2,1)S(1)}, bf16[32,4,2,1024]{3,0,2,1:T(8,128)(2,1)S(1)}, u32[]{:S(2)}, u32[]{:S(2)}) collective-permute-start(bf16[32,4,2,1024]{3,0,2,1:T(8,128)(2,1)S(1)} %broadcast_select_fusion.3), channel_id=1, source_target_pairs={{0,8},{1,9},{2,10},{3,11},{4,12},{5,13},{6,14},{7,15},{8,0},{9,1},... | collective-permute-start | bytes 1572872 | tf_op jit(solution)/shard_map/ppermute | solution.py:26
  64.2 12.8 %collective-permute-start.5 = (bf16[32,4,2,1024]{3,0,2,1:T(8,128)(2,1)S(1)}, bf16[32,4,2,1024]{3,0,2,1:T(8,128)(2,1)S(1)}, u32[]{:S(2)}, u32[]{:S(2)}) collective-permute-start(bf16[32,4,2,1024]{3,0,2,1:T(8,128)(2,1)S(1)} %broadcast_select_fusion.4), channel_id=1, source_target_pairs={{0,2},{1,3},{2,4},{3,5},{4,6},{5,7},{6,0},{7,1},{8,10},{9,11},{10,... | collective-permute-start | bytes 1572872 | tf_op jit(solution)/shard_map/ppermute | solution.py:28
  64.3 12.6 %collective-permute-start.6 = (bf16[32,4,2,1024]{3,0,2,1:T(8,128)(2,1)S(1)}, bf16[32,4,2,1024]{3,0,2,1:T(8,128)(2,1)S(1)}, u32[]{:S(2)}, u32[]{:S(2)}) collective-permute-start(bf16[32,4,2,1024]{3,0,2,1:T(8,128)(2,1)S(1)} %broadcast_select_fusion.4), channel_id=1, source_target_pairs={{0,6},{1,7},{2,0},{3,1},{4,2},{5,3},{6,4},{7,5},{8,14},{9,15},{10,... | collective-permute-start | bytes 1572872 | tf_op jit(solution)/shard_map/ppermute | solution.py:29
  77.0 11.9 %collective-permute-start.7 = (bf16[32,4,2,1024]{3,0,2,1:T(8,128)(2,1)S(1)}, bf16[32,4,2,1024]{3,0,2,1:T(8,128)(2,1)S(1)}, u32[]{:S(2)}, u32[]{:S(2)}) collective-permute-start(bf16[32,4,2,1024]{3,0,2,1:T(8,128)(2,1)S(1)} %select_select_fusion), channel_id=1, source_target_pairs={{0,2},{1,3},{2,4},{3,5},{4,6},{5,7},{6,0},{7,1},{8,10},{9,11},{10,... | collective-permute-start | bytes 1572872 | tf_op jit(solution)/shard_map/ppermute | solution.py:32
  89.8 145.1 %all-gather.5.cloned.1.call-start = ((), (), s32[]{:S(2)}) async-start(), calls=%async_computation.1 | async-start | bytes 5242880 | tf_op jit(solution)/shard_map/all_gather | solution.py:75
  153.4 112.7 %collective-permute-start.8 = (bf16[32,16,2,1024]{3,1,2,0:T(8,128)(2,1)}, bf16[32,16,2,1024]{3,1,2,0:T(8,128)(2,1)}, u32[]{:S(2)}, u32[]{:S(2)}) collective-permute-start(bf16[32,16,2,1024]{3,1,2,0:T(8,128)(2,1)} %copy.9), channel_id=1, source_target_pairs={{0,1},{1,0},{2,3},{3,2},{4,5},{5,4},{6,7},{7,6},{8,9},{9,8},{10,11... | collective-permute-start | bytes 6291464 | tf_op jit(solution)/shard_map/ppermute | solution.py:78
  247.8 6.1 %copy-start.1 = (bf16[32,16,2,1024]{3,0,2,1:T(8,128)(2,1)S(1)}, bf16[32,16,2,1024]{3,0,2,1:T(8,128)(2,1)}, u32[]{:S(2)}) copy-start(bf16[32,16,2,1024]{3,0,2,1:T(8,128)(2,1)} %all-gather.3.cloned.1.call-done) | copy-start | bytes 6291460
  290.3 20.5 %copy-start = (bf16[32,16,2,1024]{0,1,2,3:T(8,128)(2,1)}, bf16[32,16,2,1024]{0,1,2,3:T(8,128)(2,1)S(1)}, u32[]{:S(2)}) copy-start(bf16[32,16,2,1024]{0,1,2,3:T(8,128)(2,1)S(1)} %get-tuple-element.5) | copy-start | bytes 6291460
  408.6 11.8 %copy-start.3 = (bf16[1024,512]{1,0:T(8,128)(2,1)S(1)}, bf16[1024,512]{1,0:T(8,128)(2,1)}, u32[]{:S(2)}) copy-start(bf16[1024,512]{1,0:T(8,128)(2,1)} %get-tuple-element.10) | copy-start | bytes 3145732
Sparse Core Ops, SparseCore 0:
  89.9 59.3 all-gather.2
  151.1 83.6 all-gather.4
